TPU v7x, 32 devices: a whole 2x2x4 slice. The times are simulated.
32 devices in a mesh: groups: 2 (over x), seq: 16 (over z, y, core).
Axes of the slice: x: 2, y: 2, z: 4, core: 2. Of those that a mesh axis runs over, the one named last changes fastest.
Arguments:
- queries: bfloat16 [12288, 1536], P(('groups', 'seq')), parts along dimension 0, may hold values from -6 to 6
- keys: bfloat16 [12288, 1536], P(('groups', 'seq')), parts along dimension 0, may hold values from -6 to 6
- values: bfloat16 [12288, 1536], P(('groups', 'seq')), parts along dimension 0, may hold values from -6 to 6
- tile_lengths: int32 [32], P(('groups', 'seq')), parts along dimension 0, may hold values from 192 to 384
- head_windows: int32 [12, 2], replicated, may hold values from 0 to 1
- out_weight: bfloat16 [1536, 3072], P('seq'), may hold values from -0.4375 to 0.4375
- gate: float32 [6144], P('groups'), parts along dimension 0, may hold values from 0.5 to 2
Outputs:
- attn_branch: bfloat16 [12288, 3072], P(('groups', 'seq')), parts along dimension 0
There are 2 independent parts, one for each index of `groups`. A program takes and returns all parts, laid end to end along the dimension named above; an argument that names none is the same for every part. Nothing has to cross between parts.
All inputs are finite; a program needn't handle non-finite values.
Results may differ from a plain program's by a relative error of at most 0.0057.
Values may be sent and summed in bfloat16 or wider, within the bound.
No kernel may reach another device: no remote copies, remote signals or barrier semaphores. Data moves between devices by JAX's collectives and lax.ppermute only.
A program may use at most 128 MiB of HBM per device.

v0:
```python
import math

import jax
import jax.numpy as jnp
from jax import lax
from jax.sharding import PartitionSpec as P

TW = 8


OFFSETS = ((-1, -1), (-1, 0), (-1, 1), (0, -1), (0, 0), (0, 1), (1, -1), (1, 0), (1, 1))


def passed_along(shard, axis, by):
    peers = lax.axis_size(axis)
    pairs = [(i, i + by) for i in range(peers) if 0 <= i + by < peers]
    return lax.ppermute(shard, axis, pairs)


def attend(query_block, head_keys, head_values, usable, score_scale):
    scores = (
        lax.dot_general(
            query_block, head_keys, (((1,), (1,)), ((), ())), preferred_element_type=jnp.float32
        )
        * score_scale
    )
    scores = jnp.where(usable[None, :], scores, -1e30)
    maximum = jnp.max(scores, axis=1, keepdims=True)
    exponent = jnp.where(usable[None, :], jnp.exp(scores - maximum), 0.0)
    denominator = jnp.sum(exponent, axis=1, keepdims=True)
    weights = (exponent / denominator).astype(jnp.bfloat16)
    return jnp.dot(weights, head_values, preferred_element_type=jnp.float32)


def on_device(queries, keys, values, tile_lengths, head_windows, out_weight, gate):
    devices = lax.axis_size("seq")
    device_index = lax.axis_index("seq")
    grid_rows = devices // TW
    grid_row = device_index // TW
    grid_col = device_index % TW
    tile_rows = queries.shape[0]
    feat_width = queries.shape[1]
    head_count = head_windows.shape[0]
    head_dim = feat_width // head_count
    score_scale = 1.0 / math.sqrt(head_dim)
    key_list = []
    value_list = []
    length_list = []
    for row_step, col_step in OFFSETS:
        if row_step == 0 and col_step == 0:
            key_list.append(keys)
            value_list.append(values)
            length_list.append(tile_lengths)
        else:
            got_keys, got_values, got_lengths = passed_along(
                (keys, values, tile_lengths), "seq", -(row_step * TW + col_step)
            )
            key_list.append(got_keys)
            value_list.append(got_values)
            length_list.append(
                jnp.where(
                    (grid_row + row_step >= 0)
                    & (grid_row + row_step < grid_rows)
                    & (grid_col + col_step >= 0)
                    & (grid_col + col_step < TW),
                    got_lengths,
                    0,
                )
            )
    key_stack = jnp.stack(key_list)
    value_stack = jnp.stack(value_list)
    length_stack = jnp.concatenate(length_list)
    key_flat = key_stack.reshape(9 * tile_rows, feat_width)
    value_flat = value_stack.reshape(9 * tile_rows, feat_width)
    positions = jnp.arange(tile_rows, dtype=jnp.int32)
    key_real = positions[None, :] < length_stack[:, None]
    query_real = positions < tile_lengths[0]
    far_rows = jnp.array([abs(pair[0]) for pair in OFFSETS], jnp.int32)
    far_cols = jnp.array([abs(pair[1]) for pair in OFFSETS], jnp.int32)

    def one_head(head_index, attended_all):
        offset = head_index * head_dim
        query_block = lax.dynamic_slice_in_dim(queries, offset, head_dim, 1)
        head_keys = lax.dynamic_slice_in_dim(key_flat, offset, head_dim, 1)
        head_values = lax.dynamic_slice_in_dim(value_flat, offset, head_dim, 1)
        reach_rows = head_windows[head_index, 0]
        reach_cols = head_windows[head_index, 1]
        window = (far_rows <= reach_rows) & (far_cols <= reach_cols)
        usable = (key_real & window[:, None]).reshape(-1)
        attended = attend(query_block, head_keys, head_values, usable, score_scale)
        attended = jnp.where(query_real[:, None], attended, 0.0).astype(jnp.bfloat16)
        return lax.dynamic_update_slice_in_dim(attended_all, attended, offset, 1)

    attended_all = lax.fori_loop(
        0, head_count, one_head, jnp.zeros((tile_rows, feat_width), jnp.bfloat16)
    )
    projected = jnp.dot(
        attended_all,
        lax.all_gather(out_weight, "seq", axis=0, tiled=True),
        preferred_element_type=jnp.float32,
    )
    return (projected * gate[None, :]).astype(jnp.bfloat16)


def solution(mesh):
    placed = (
        P(("groups", "seq"), None),
        P(("groups", "seq"), None),
        P(("groups", "seq"), None),
        P(("groups", "seq")),
        P(),
        P("seq", None),
        P("groups"),
    )
    return jax.shard_map(
        on_device, mesh=mesh, in_specs=placed, out_specs=P(("groups", "seq"), None), check_vma=False
    )
```

profile of v0, /device:TPU:0, one launch (start us, length us, event | category | flops | bytes accessed | tf_op | source)
XLA Modules:
  0.0 702.7 jit_solution(11108539776981291992)
XLA Ops:
  6.5 6.6 collective-permute-start.16
  13.1 2.3 collective-permute-start.17
  15.4 3.2 collective-permute-start.18
  23.1 84.3 %collective-permute-done = s32[1]{0:T(128)} collective-permute-done((s32[1]{0:T(128)}, s32[1]{0:T(128)}, u32[]{:S(2)}, u32[]{:S(2)}) %collective-permute-start) | collective-permute-done | bytes 36 | tf_op jit(solution)/shard_map/ppermute | solution.py:17
  113.2 106.5 %collective-permute-start.1 = (s32[1]{0:T(128)}, s32[1]{0:T(128)}, u32[]{:S(2)}, u32[]{:S(2)}) collective-permute-start(s32[1]{0:T(128)} %param.14), channel_id=1, source_target_pairs={{0,8},{1,9},{2,10},{3,11},{4,12},{5,13},{6,14},{7,15},{16,24},{17,... | collective-permute-start | bytes 20 | tf_op jit(solution)/shard_map/ppermute | solution.py:17
  226.7 4.8 collective-permute-start.19
  236.9 8.5 %collective-permute-start.8 = (bf16[384,1536]{1,0:T(8,128)(2,1)}, bf16[384,1536]{1,0:T(8,128)(2,1)S(1)}, u32[]{:S(2)}, u32[]{:S(2)}) collective-permute-start(bf16[384,1536]{1,0:T(8,128)(2,1)} %param.12), channel_id=1, source_target_pairs={{0,9},{1,10},{2,11},{3,12},{4,13},{5,14},{6,15},{16,25},{17,26},{1... | collective-permute-start | bytes 3538952 | tf_op jit(solution)/shard_map/ppermute | solution.py:17
  248.2 81.4 %collective-permute-start.10 = (bf16[384,1536]{1,0:T(8,128)(2,1)S(1)}, bf16[384,1536]{1,0:T(8,128)(2,1)S(1)}, u32[]{:S(2)}, u32[]{:S(2)}) collective-permute-start(bf16[384,1536]{1,0:T(8,128)(2,1)S(1)} %copy-done.2), channel_id=1, source_target_pairs={{0,7},{1,8},{2,9},{3,10},{4,11},{5,12},{6,13},{7,14},{8,15},{16,23... | collective-permute-start | bytes 3538952 | tf_op jit(solution)/shard_map/ppermute | solution.py:17
  331.1 4.3 collective-permute-start.11
  336.8 17.4 %collective-permute-done.10 = bf16[384,1536]{1,0:T(8,128)(2,1)S(1)} collective-permute-done((bf16[384,1536]{1,0:T(8,128)(2,1)S(1)}, bf16[384,1536]{1,0:T(8,128)(2,1)S(1)}, u32[]{:S(2)}, u32[]{:S(2)}) %collective-permute-start.10) | collective-permute-done | bytes 1179680 | tf_op jit(solution)/shard_map/ppermute | solution.py:17
  361.2 31.3 %collective-permute-done.22 = bf16[384,1536]{1,0:T(8,128)(2,1)S(1)} collective-permute-done((bf16[384,1536]{1,0:T(8,128)(2,1)S(1)}, bf16[384,1536]{1,0:T(8,128)(2,1)S(1)}, u32[]{:S(2)}, u32[]{:S(2)}) %collective-permute-start.22) | collective-permute-done | bytes 1179680 | tf_op jit(solution)/shard_map/ppermute | solution.py:17
  393.8 121.6 %collective-permute-done.23 = bf16[384,1536]{1,0:T(8,128)(2,1)S(1)} collective-permute-done((bf16[384,1536]{1,0:T(8,128)(2,1)S(1)}, bf16[384,1536]{1,0:T(8,128)(2,1)S(1)}, u32[]{:S(2)}, u32[]{:S(2)}) %collective-permute-start.23) | collective-permute-done | bytes 1179680 | tf_op jit(solution)/shard_map/ppermute | solution.py:17
  515.8 54.9 %collective-permute-done.14 = bf16[384,1536]{1,0:T(8,128)(2,1)S(1)} collective-permute-done((bf16[384,1536]{1,0:T(8,128)(2,1)S(1)}, bf16[384,1536]{1,0:T(8,128)(2,1)S(1)}, u32[]{:S(2)}, u32[]{:S(2)}) %collective-permute-start.14) | collective-permute-done | bytes 1179680 | tf_op jit(solution)/shard_map/ppermute | solution.py:17
  570.7 10.2 %collective-permute-done.15 = bf16[384,1536]{1,0:T(8,128)(2,1)S(1)} collective-permute-done((bf16[384,1536]{1,0:T(8,128)(2,1)S(1)}, bf16[384,1536]{1,0:T(8,128)(2,1)S(1)}, u32[]{:S(2)}, u32[]{:S(2)}) %collective-permute-start.15) | collective-permute-done | bytes 1179680 | tf_op jit(solution)/shard_map/ppermute | solution.py:17
  581.2 4.0 copy-done
  585.1 101.9 %while.15 = (s32[]{:T(128)}, bf16[384,1536]{1,0:T(8,128)(2,1)S(1)}, s32[12,2]{0,1:T(2,128)S(1)}, bf16[384,1536]{1,0:T(8,128)(2,1)}, bf16[3456,1536]{1,0:T(8,128)...) while((s32[]{:T(128)}, bf16[384,1536]{1,0:T(8,128)(2,1)S(1)}, ...), condition=%wide.region_3.4_spmd.clone.clone, body=%wide.region_0.3_spmd.sunk.clone.clone.sunk | while | flops 692853120 | bytes 17924688 | solution.py:94
  587.2 2.3 fusion.27
  591.3 2.4 fusion.29
  599.8 2.4 fusion.29
  604.2 2.3 fusion.27
  608.3 2.4 fusion.29
  616.8 2.4 fusion.29
  625.2 2.4 fusion.29
  629.7 2.3 fusion.27
  633.7 2.4 fusion.29
  642.2 2.4 fusion.29
  650.7 2.4 fusion.29
  659.2 2.4 fusion.29
  667.7 2.4 fusion.29
  676.2 2.4 fusion.29
  684.7 2.4 fusion.29
  687.1 8.7 %multiply_convert_fusion = bf16[384,3072]{1,0:T(8,128)(2,1)} fusion(bf16[384,1536]{1,0:T(8,128)(2,1)S(1)} %get-tuple-element.174, bf16[1536,3072]{1,0:T(8,128)(2,1)} %all-gather.2.cloned.1.call-done, f32[3072]{0:T(1024)S(1)} %copy-done.7), kind=kOutput, calls=%fused_computation.23 | convolution fusion | flops 3626237952 | bytes 12988416 | tf_op jit(solution)/shard_map/dot_general | solution.py:97
  (153 shorter events, 97.2 us)
Async XLA Ops:
  6.5 324.4 %copy-start.1 = (bf16[384,1536]{1,0:T(8,128)(2,1)S(1)}, bf16[384,1536]{1,0:T(8,128)(2,1)}, u32[]{:S(2)}) copy-start(bf16[384,1536]{1,0:T(8,128)(2,1)} %param.13) | copy-start | bytes 3538948
  6.5 240.2 %copy-start.2 = (bf16[384,1536]{1,0:T(8,128)(2,1)S(1)}, bf16[384,1536]{1,0:T(8,128)(2,1)}, u32[]{:S(2)}) copy-start(bf16[384,1536]{1,0:T(8,128)(2,1)} %param.12) | copy-start | bytes 3538948
  6.5 680.5 %all-gather.2.cloned.1.call-start = ((), (), s32[]{:S(2)}) async-start(), calls=%async_computation | async-start | bytes 10027008 | tf_op jit(solution)/shard_map/all_gather | solution.py:99
  6.5 227.7 %collective-permute-start.16 = (bf16[384,1536]{1,0:T(8,128)(2,1)}, bf16[384,1536]{1,0:T(8,128)(2,1)}, u32[]{:S(2)}, u32[]{:S(2)}) collective-permute-start(bf16[384,1536]{1,0:T(8,128)(2,1)} %param.13), channel_id=1, source_target_pairs={{0,9},{1,10},{2,11},{3,12},{4,13},{5,14},{6,15},{16,25},{17,26},{1... | collective-permute-start | bytes 3538952 | tf_op jit(solution)/shard_map/ppermute | solution.py:17
  13.1 223.8 %collective-permute-start.17 = (bf16[384,1536]{1,0:T(8,128)(2,1)}, bf16[384,1536]{1,0:T(8,128)(2,1)}, u32[]{:S(2)}, u32[]{:S(2)}) collective-permute-start(bf16[384,1536]{1,0:T(8,128)(2,1)} %param.13), channel_id=1, source_target_pairs={{0,8},{1,9},{2,10},{3,11},{4,12},{5,13},{6,14},{7,15},{16,24},{17,... | collective-permute-start | bytes 3538952 | tf_op jit(solution)/shard_map/ppermute | solution.py:17
  15.4 231.3 %collective-permute-start.18 = (bf16[384,1536]{1,0:T(8,128)(2,1)}, bf16[384,1536]{1,0:T(8,128)(2,1)S(1)}, u32[]{:S(2)}, u32[]{:S(2)}) collective-permute-start(bf16[384,1536]{1,0:T(8,128)(2,1)} %param.13), channel_id=1, source_target_pairs={{0,7},{1,8},{2,9},{3,10},{4,11},{5,12},{6,13},{7,14},{8,15},{16,23... | collective-permute-start | bytes 3538952 | tf_op jit(solution)/shard_map/ppermute | solution.py:17
  18.7 88.7 %collective-permute-start = (s32[1]{0:T(128)}, s32[1]{0:T(128)}, u32[]{:S(2)}, u32[]{:S(2)}) collective-permute-start(s32[1]{0:T(128)} %param.14), channel_id=1, source_target_pairs={{0,9},{1,10},{2,11},{3,12},{4,13},{5,14},{6,15},{16,25},{17,26},{1... | collective-permute-start | bytes 20 | tf_op jit(solution)/shard_map/ppermute | solution.py:17
  20.5 88.8 %collective-permute-start.2 = (s32[1]{0:T(128)}, s32[1]{0:T(128)}, u32[]{:S(2)}, u32[]{:S(2)}) collective-permute-start(s32[1]{0:T(128)} %param.14), channel_id=1, source_target_pairs={{0,7},{1,8},{2,9},{3,10},{4,11},{5,12},{6,13},{7,14},{8,15},{16,23... | collective-permute-start | bytes 20 | tf_op jit(solution)/shard_map/ppermute | solution.py:17
  107.4 5.9 collective-permute-start.5
  109.2 111.2 %collective-permute-start.7 = (s32[1]{0:T(128)}, s32[1]{0:T(128)}, u32[]{:S(2)}, u32[]{:S(2)}) collective-permute-start(s32[1]{0:T(128)} %param.14), channel_id=1, source_target_pairs={{9,0},{10,1},{11,2},{12,3},{13,4},{14,5},{15,6},{25,16},{26,17},{2... | collective-permute-start | bytes 20 | tf_op jit(solution)/shard_map/ppermute | solution.py:17
  113.2 109.6 %collective-permute-start.1 = (s32[1]{0:T(128)}, s32[1]{0:T(128)}, u32[]{:S(2)}, u32[]{:S(2)}) collective-permute-start(s32[1]{0:T(128)} %param.14), channel_id=1, source_target_pairs={{0,8},{1,9},{2,10},{3,11},{4,12},{5,13},{6,14},{7,15},{16,24},{17,... | collective-permute-start | bytes 20 | tf_op jit(solution)/shard_map/ppermute | solution.py:17
  220.4 4.4 collective-permute-start.3
  222.8 3.9 collective-permute-start.4
  224.8 7.3 %collective-permute-start.6 = (s32[1]{0:T(128)}, s32[1]{0:T(128)}, u32[]{:S(2)}, u32[]{:S(2)}) collective-permute-start(s32[1]{0:T(128)} %param.14), channel_id=1, source_target_pairs={{8,0},{9,1},{10,2},{11,3},{12,4},{13,5},{14,6},{15,7},{24,16},{25,... | collective-permute-start | bytes 20 | tf_op jit(solution)/shard_map/ppermute | solution.py:17
  226.7 21.5 %collective-permute-start.19 = (bf16[384,1536]{1,0:T(8,128)(2,1)}, bf16[384,1536]{1,0:T(8,128)(2,1)}, u32[]{:S(2)}, u32[]{:S(2)}) collective-permute-start(bf16[384,1536]{1,0:T(8,128)(2,1)} %param.13), channel_id=1, source_target_pairs={{0,1},{1,2},{2,3},{3,4},{4,5},{5,6},{6,7},{7,8},{8,9},{9,10},{10,1... | collective-permute-start | bytes 3538952 | tf_op jit(solution)/shard_map/ppermute | solution.py:17
  232.1 125.0 %collective-permute-start.20 = (bf16[384,1536]{1,0:T(8,128)(2,1)}, bf16[384,1536]{1,0:T(8,128)(2,1)}, u32[]{:S(2)}, u32[]{:S(2)}) collective-permute-start(bf16[384,1536]{1,0:T(8,128)(2,1)} %param.13), channel_id=1, source_target_pairs={{1,0},{2,1},{3,2},{4,3},{5,4},{6,5},{7,6},{8,7},{9,8},{10,9},{11,1... | collective-permute-start | bytes 3538952 | tf_op jit(solution)/shard_map/ppermute | solution.py:17
  234.2 125.5 %collective-permute-start.21 = (bf16[384,1536]{1,0:T(8,128)(2,1)}, bf16[384,1536]{1,0:T(8,128)(2,1)S(1)}, u32[]{:S(2)}, u32[]{:S(2)}) collective-permute-start(bf16[384,1536]{1,0:T(8,128)(2,1)} %param.13), channel_id=1, source_target_pairs={{7,0},{8,1},{9,2},{10,3},{11,4},{12,5},{13,6},{14,7},{15,8},{23,16... | collective-permute-start | bytes 3538952 | tf_op jit(solution)/shard_map/ppermute | solution.py:17
  236.9 94.2 %collective-permute-start.8 = (bf16[384,1536]{1,0:T(8,128)(2,1)}, bf16[384,1536]{1,0:T(8,128)(2,1)S(1)}, u32[]{:S(2)}, u32[]{:S(2)}) collective-permute-start(bf16[384,1536]{1,0:T(8,128)(2,1)} %param.12), channel_id=1, source_target_pairs={{0,9},{1,10},{2,11},{3,12},{4,13},{5,14},{6,15},{16,25},{17,26},{1... | collective-permute-start | bytes 3538952 | tf_op jit(solution)/shard_map/ppermute | solution.py:17
  246.7 88.7 %collective-permute-start.9 = (bf16[384,1536]{1,0:T(8,128)(2,1)S(1)}, bf16[384,1536]{1,0:T(8,128)(2,1)S(1)}, u32[]{:S(2)}, u32[]{:S(2)}) collective-permute-start(bf16[384,1536]{1,0:T(8,128)(2,1)S(1)} %copy-done.2), channel_id=1, source_target_pairs={{0,8},{1,9},{2,10},{3,11},{4,12},{5,13},{6,14},{7,15},{16,24},{17,... | collective-permute-start | bytes 3538952 | tf_op jit(solution)/shard_map/ppermute | solution.py:17
  248.2 106.0 %collective-permute-start.10 = (bf16[384,1536]{1,0:T(8,128)(2,1)S(1)}, bf16[384,1536]{1,0:T(8,128)(2,1)S(1)}, u32[]{:S(2)}, u32[]{:S(2)}) collective-permute-start(bf16[384,1536]{1,0:T(8,128)(2,1)S(1)} %copy-done.2), channel_id=1, source_target_pairs={{0,7},{1,8},{2,9},{3,10},{4,11},{5,12},{6,13},{7,14},{8,15},{16,23... | collective-permute-start | bytes 3538952 | tf_op jit(solution)/shard_map/ppermute | solution.py:17
  331.1 24.6 %collective-permute-start.11 = (bf16[384,1536]{1,0:T(8,128)(2,1)S(1)}, bf16[384,1536]{1,0:T(8,128)(2,1)S(1)}, u32[]{:S(2)}, u32[]{:S(2)}) collective-permute-start(bf16[384,1536]{1,0:T(8,128)(2,1)S(1)} %copy-done.2), channel_id=1, source_target_pairs={{0,1},{1,2},{2,3},{3,4},{4,5},{5,6},{6,7},{7,8},{8,9},{9,10},{10,1... | collective-permute-start | bytes 3538952 | tf_op jit(solution)/shard_map/ppermute | solution.py:17
  335.5 57.0 %collective-permute-start.22 = (bf16[384,1536]{1,0:T(8,128)(2,1)S(1)}, bf16[384,1536]{1,0:T(8,128)(2,1)S(1)}, u32[]{:S(2)}, u32[]{:S(2)}) collective-permute-start(bf16[384,1536]{1,0:T(8,128)(2,1)S(1)} %copy-done.1), channel_id=1, source_target_pairs={{8,0},{9,1},{10,2},{11,3},{12,4},{13,5},{14,6},{15,7},{24,16},{25,... | collective-permute-start | bytes 3538952 | tf_op jit(solution)/shard_map/ppermute | solution.py:17
  354.2 161.2 %collective-permute-start.23 = (bf16[384,1536]{1,0:T(8,128)(2,1)S(1)}, bf16[384,1536]{1,0:T(8,128)(2,1)S(1)}, u32[]{:S(2)}, u32[]{:S(2)}) collective-permute-start(bf16[384,1536]{1,0:T(8,128)(2,1)S(1)} %copy-done.1), channel_id=1, source_target_pairs={{9,0},{10,1},{11,2},{12,3},{13,4},{14,5},{15,6},{25,16},{26,17},{2... | collective-permute-start | bytes 3538952 | tf_op jit(solution)/shard_map/ppermute | solution.py:17
  355.6 160.0 %collective-permute-start.12 = (bf16[384,1536]{1,0:T(8,128)(2,1)S(1)}, bf16[384,1536]{1,0:T(8,128)(2,1)S(1)}, u32[]{:S(2)}, u32[]{:S(2)}) collective-permute-start(bf16[384,1536]{1,0:T(8,128)(2,1)S(1)} %copy-done.2), channel_id=1, source_target_pairs={{1,0},{2,1},{3,2},{4,3},{5,4},{6,5},{7,6},{8,7},{9,8},{10,9},{11,1... | collective-permute-start | bytes 3538952 | tf_op jit(solution)/shard_map/ppermute | solution.py:17
  357.1 158.6 %collective-permute-start.13 = (bf16[384,1536]{1,0:T(8,128)(2,1)S(1)}, bf16[384,1536]{1,0:T(8,128)(2,1)S(1)}, u32[]{:S(2)}, u32[]{:S(2)}) collective-permute-start(bf16[384,1536]{1,0:T(8,128)(2,1)S(1)} %copy-done.2), channel_id=1, source_target_pairs={{7,0},{8,1},{9,2},{10,3},{11,4},{12,5},{13,6},{14,7},{15,8},{23,16... | collective-permute-start | bytes 3538952 | tf_op jit(solution)/shard_map/ppermute | solution.py:17
  359.8 210.9 %collective-permute-start.14 = (bf16[384,1536]{1,0:T(8,128)(2,1)S(1)}, bf16[384,1536]{1,0:T(8,128)(2,1)S(1)}, u32[]{:S(2)}, u32[]{:S(2)}) collective-permute-start(bf16[384,1536]{1,0:T(8,128)(2,1)S(1)} %copy-done.2), channel_id=1, source_target_pairs={{8,0},{9,1},{10,2},{11,3},{12,4},{13,5},{14,6},{15,7},{24,16},{25,... | collective-permute-start | bytes 3538952 | tf_op jit(solution)/shard_map/ppermute | solution.py:17
  392.5 188.5 %collective-permute-start.15 = (bf16[384,1536]{1,0:T(8,128)(2,1)S(1)}, bf16[384,1536]{1,0:T(8,128)(2,1)S(1)}, u32[]{:S(2)}, u32[]{:S(2)}) collective-permute-start(bf16[384,1536]{1,0:T(8,128)(2,1)S(1)} %copy-done.2), channel_id=1, source_target_pairs={{9,0},{10,1},{11,2},{12,3},{13,4},{14,5},{15,6},{25,16},{26,17},{2... | collective-permute-start | bytes 3538952 | tf_op jit(solution)/shard_map/ppermute | solution.py:17
  515.5 65.6 %copy-start.3 = (bf16[9,384,1536]{2,1,0:T(8,128)(2,1)}, bf16[9,384,1536]{2,1,0:T(8,128)(2,1)S(1)}, u32[]{:S(2)}) copy-start(bf16[9,384,1536]{2,1,0:T(8,128)(2,1)S(1)} %bitcast_dynamic-update-slice_fusion) | copy-start | bytes 31850500
  515.5 69.6 %copy-start.4 = (s32[12,2]{0,1:T(2,128)S(1)}, s32[12,2]{0,1:T(2,128)}, u32[]{:S(2)}) copy-start(s32[12,2]{0,1:T(2,128)} %param.15) | copy-start | bytes 292
  515.6 69.6 %copy-start.5 = (s32[9]{0:T(128)S(1)}, s32[9]{0:T(128)}, u32[]{:S(2)}) copy-start(s32[9]{0:T(128)} %constant.101.clone..sunk.3) | copy-start | bytes 112
  515.6 69.6 %copy-start.6 = (s32[9]{0:T(128)S(1)}, s32[9]{0:T(128)}, u32[]{:S(2)}) copy-start(s32[9]{0:T(128)} %constant.102.clone..sunk.3) | copy-start | bytes 112
  585.1 101.9 %copy-start.7 = (f32[3072]{0:T(1024)S(1)}, f32[3072]{0:T(1024)}, u32[]{:S(2)}) copy-start(f32[3072]{0:T(1024)} %param.17) | copy-start | bytes 36868
  (1 other events, 4.1 us)
Sparse Core Ops, SparseCore 0:
  22.5 147.3 all-gather.1
where the time goes:
time: 705 us; the launch traced here: 703 us
  waiting for transfers between devices  322 us (46%)
  starting transfers between devices  240 us (34%)
  matrix products  64.4 us (9%)
  other arithmetic  37.6 us (5%)
  between operations  19.7 us (3%)
  local copies, waits for them, and re-layouts  18.7 us (3%)
    ppermute x24, waiting for transfers between devices, passed_along(): return lax.ppermute(shard, axis, pairs)  322 us
    ppermute x24, starting transfers between devices, passed_along(): return lax.ppermute(shard, axis, pairs)  240 us
    dot_general x12, matrix products, attend(): return jnp.dot(weights, head_values, preferred_element_type=jnp.float32)  28.5 us
    dot_general x12, matrix products, attend(): lax.dot_general(query_block, head_keys, (((1,), (1,)), ((), ())), preferr...  27.2 us
    and x12, other arithmetic, one_head(): window = (far_rows <= reach_rows) & (far_cols <= reach_cols)  15.8 us
  transfers between devices with their start and end apart: 25, of which 7 were waited for; matrix products, arithmetic and copies ran while one was open for 15% of the time, Pallas kernels for 0%

commit v1 on v0

v1 whole, which is shorter than its diff:
```python
import math

import jax
import jax.numpy as jnp
from jax import lax
from jax.sharding import PartitionSpec as P

TW = 8


def attend(query_block, head_keys, head_values, usable, score_scale):
    scores = (
        lax.dot_general(
            query_block, head_keys, (((1,), (1,)), ((), ())), preferred_element_type=jnp.float32
        )
        * score_scale
    )
    scores = jnp.where(usable[None, :], scores, -1e30)
    maximum = jnp.max(scores, axis=1, keepdims=True)
    exponent = jnp.where(usable[None, :], jnp.exp(scores - maximum), 0.0)
    denominator = jnp.sum(exponent, axis=1, keepdims=True)
    weights = (exponent / denominator).astype(jnp.bfloat16)
    return jnp.dot(weights, head_values, preferred_element_type=jnp.float32)


def vertical_parts(devices, grid_rows):
    if grid_rows == 1:
        return []
    down = [(i, i + TW) for i in range(devices - TW)]
    up = [(i + TW, i) for i in range(devices - TW)]
    if grid_rows == 2:
        return [down + up]
    return [down, up]


def on_device(queries, keys, values, tile_lengths, head_windows, out_weight, gate):
    devices = lax.axis_size("seq")
    grid_rows = devices // TW
    tile_rows = queries.shape[0]
    feat_width = queries.shape[1]
    head_count = head_windows.shape[0]
    head_dim = feat_width // head_count
    score_scale = 1.0 / math.sqrt(head_dim)

    pair = jnp.concatenate([keys, values], axis=1)
    column = [pair]
    column_lengths = [tile_lengths]
    column_rows = [0]
    for pairs in vertical_parts(devices, grid_rows):
        got, got_lengths = lax.ppermute((pair, tile_lengths), "seq", pairs)
        column.append(got)
        column_lengths.append(got_lengths)
        column_rows.append(1)
    column = jnp.stack(column)
    column_lengths = jnp.concatenate(column_lengths)

    to_right = [(i, i + 1) for i in range(devices) if i % TW < TW - 1]
    to_left = [(i + 1, i) for i in range(devices) if i % TW < TW - 1]
    from_left = lax.ppermute((column, column_lengths), "seq", to_right)
    from_right = lax.ppermute((column, column_lengths), "seq", to_left)

    slots = len(column_rows)
    key_stack = jnp.concatenate([column, from_left[0], from_right[0]])
    length_stack = jnp.concatenate([column_lengths, from_left[1], from_right[1]])
    far_rows = jnp.array(column_rows * 3, jnp.int32)
    far_cols = jnp.array([0] * slots + [1] * slots + [1] * slots, jnp.int32)
    key_flat = key_stack.reshape(3 * slots * tile_rows, 2 * feat_width)

    positions = jnp.arange(tile_rows, dtype=jnp.int32)
    key_real = positions[None, :] < length_stack[:, None]
    query_real = positions < tile_lengths[0]

    def one_head(head_index, attended_all):
        offset = head_index * head_dim
        query_block = lax.dynamic_slice_in_dim(queries, offset, head_dim, 1)
        head_keys = lax.dynamic_slice_in_dim(key_flat, offset, head_dim, 1)
        head_values = lax.dynamic_slice_in_dim(key_flat, feat_width + offset, head_dim, 1)
        reach_rows = head_windows[head_index, 0]
        reach_cols = head_windows[head_index, 1]
        window = (far_rows <= reach_rows) & (far_cols <= reach_cols)
        usable = (key_real & window[:, None]).reshape(-1)
        attended = attend(query_block, head_keys, head_values, usable, score_scale)
        attended = jnp.where(query_real[:, None], attended, 0.0).astype(jnp.bfloat16)
        return lax.dynamic_update_slice_in_dim(attended_all, attended, offset, 1)

    attended_all = lax.fori_loop(
        0, head_count, one_head, jnp.zeros((tile_rows, feat_width), jnp.bfloat16)
    )
    projected = jnp.dot(
        attended_all,
        lax.all_gather(out_weight, "seq", axis=0, tiled=True),
        preferred_element_type=jnp.float32,
    )
    return (projected * gate[None, :]).astype(jnp.bfloat16)


def solution(mesh):
    placed = (
        P(("groups", "seq"), None),
        P(("groups", "seq"), None),
        P(("groups", "seq"), None),
        P(("groups", "seq")),
        P(),
        P("seq", None),
        P("groups"),
    )
    return jax.shard_map(
        on_device, mesh=mesh, in_specs=placed, out_specs=P(("groups", "seq"), None), check_vma=False
    )
```

time: 705 us -> 400 us (0.57)
  the two profiles are of different devices: /device:TPU:0 before, /device:TPU:27 now
where the time goes in v1:
time: 400 us; the launch traced here: 398 us
  waiting for transfers between devices  140 us (35%)
  starting transfers between devices  102 us (26%)
  other arithmetic  66.3 us (17%)
  matrix products  63.4 us (16%)
  between operations  14.1 us (4%)
  local copies, waits for them, and re-layouts  12.1 us (3%)
    ppermute x2, waiting for transfers between devices, on_device(): got, got_lengths = lax.ppermute((pair, tile_lengths), 'seq', pairs)  108 us
    ppermute x2, starting transfers between devices, on_device(): from_right = lax.ppermute((column, column_lengths), 'seq', to_left)  93.6 us
    ppermute x2, waiting for transfers between devices, on_device(): from_right = lax.ppermute((column, column_lengths), 'seq', to_left)  32.4 us
    dot_general x12, matrix products, attend(): return jnp.dot(weights, head_values, preferred_element_type=jnp.float32)  31.6 us
    and x12, other arithmetic, one_head(): window = (far_rows <= reach_rows) & (far_cols <= reach_cols)  23.9 us
    dot_general x12, matrix products, attend(): lax.dot_general(query_block, head_keys, (((1,), (1,)), ((), ())), preferr...  22.6 us
    concatenate x1, other arithmetic, on_device(): key_stack = jnp.concatenate([column, from_left[0], from_right[0]])  11.9 us
    dot_general x1, matrix products, on_device(): jnp.dot(attended_all, lax.all_gather(out_weight, 'seq', axis=0, tiled=Tru...  9.18 us
  transfers between devices with their start and end apart: 7, of which 3 were waited for; matrix products, arithmetic and copies ran while one was open for 32% of the time, Pallas kernels for 0%

profile of v1, /device:TPU:27, one launch (start us, length us, event | category | flops | bytes accessed | tf_op | source)
XLA Modules:
  0.0 397.9 jit_solution(8530490400043742698)
XLA Ops:
  9.5 104.5 %collective-permute-done.3 = bf16[384,3072]{1,0:T(8,128)(2,1)S(1)} collective-permute-done((bf16[384,3072]{1,0:T(8,128)(2,1)S(1)}, bf16[384,3072]{1,0:T(8,128)(2,1)S(1)}, u32[]{:S(2)}, u32[]{:S(2)}) %collective-permute-start.3) | collective-permute-done | bytes 2359328 | tf_op jit(solution)/shard_map/ppermute | solution.py:50
  114.0 2.8 pad_maximum_fusion.1
  116.9 3.5 collective-permute-start.4
  123.2 3.2 collective-permute-done
  127.1 4.3 %collective-permute-start.1 = (s32[2]{0:T(128)S(1)}, s32[2]{0:T(128)S(1)}, u32[]{:S(2)}, u32[]{:S(2)}) collective-permute-start(s32[2]{0:T(128)S(1)} %pad_add_fusion), channel_id=1, source_target_pairs={{0,1},{1,2},{2,3},{3,4},{4,5},{5,6},{6,7},{8,9},{9,10},{10,11},{11... | collective-permute-start | bytes 32 | tf_op jit(solution)/shard_map/ppermute | solution.py:59
  131.4 91.7 %collective-permute-start.2 = (s32[2]{0:T(128)S(1)}, s32[2]{0:T(128)S(1)}, u32[]{:S(2)}, u32[]{:S(2)}) collective-permute-start(s32[2]{0:T(128)S(1)} %pad_add_fusion), channel_id=1, source_target_pairs={{1,0},{2,1},{3,2},{4,3},{5,4},{6,5},{7,6},{9,8},{10,9},{11,10},{12... | collective-permute-start | bytes 32 | tf_op jit(solution)/shard_map/ppermute | solution.py:60
  223.2 32.4 %collective-permute-done.2 = s32[2]{0:T(128)S(1)} collective-permute-done((s32[2]{0:T(128)S(1)}, s32[2]{0:T(128)S(1)}, u32[]{:S(2)}, u32[]{:S(2)}) %collective-permute-start.2) | collective-permute-done | bytes 40 | tf_op jit(solution)/shard_map/ppermute | solution.py:60
  256.9 11.9 %pad_maximum_fusion = bf16[6,384,3072]{2,1,0:T(8,128)(2,1)} fusion(bf16[2,384,3072]{2,1,0:T(8,128)(2,1)} %collective-permute-done.5, bf16[2,384,3072]{2,1,0:T(8,128)(2,1)} %collective-permute-done.4, bf16[1,384,3072]{2,1,0:T(8,128)(2,1)} %bitcast.16, bf16[1,384,3072]{2,1,0:T(8,128)(2,1)S(1)} %bitcast.14), kind=kLoop, calls=%fused_computation.23 | loop fusion | flops 21233664 | bytes 28311552 | tf_op jit(solution)/shard_map/concatenate | solution.py:63
  270.0 111.9 %while.17 = (s32[]{:T(128)}, bf16[384,1536]{1,0:T(8,128)(2,1)}, s32[12,2]{0,1:T(2,128)S(1)}, bf16[384,1536]{1,0:T(8,128)(2,1)}, bf16[2304,3072]{1,0:T(8,128)(2,1...) while((s32[]{:T(128)}, bf16[384,1536]{1,0:T(8,128)(2,1)}, ...), condition=%wide.region_3.4_spmd.clone.clone, body=%wide.region_0.3_spmd.sunk.clone.clone.sunk | while | flops 461934752 | bytes 12015738 | solution.py:86
  270.6 2.0 compare_and_fusion.2
  276.6 2.6 fusion.29
  279.9 2.0 compare_and_fusion.2
  286.0 2.6 fusion.29
  289.2 2.0 compare_and_fusion.2
  295.3 2.6 fusion.29
  298.6 2.0 compare_and_fusion.2
  304.6 2.6 fusion.29
  307.9 2.0 compare_and_fusion.2
  313.9 2.6 fusion.29
  317.2 2.0 compare_and_fusion.2
  323.3 2.6 fusion.29
  326.5 2.0 compare_and_fusion.2
  332.6 2.6 fusion.29
  341.9 2.6 fusion.29
  345.2 2.0 compare_and_fusion.2
  351.2 2.6 fusion.29
  354.5 2.0 compare_and_fusion.2
  360.6 2.6 fusion.29
  369.9 2.6 fusion.29
  373.2 2.0 compare_and_fusion.2
  379.2 2.6 fusion.29
  381.9 9.2 %multiply_convert_fusion = bf16[384,3072]{1,0:T(8,128)(2,1)} fusion(bf16[384,1536]{1,0:T(8,128)(2,1)} %get-tuple-element.225, bf16[1536,3072]{1,0:T(8,128)(2,1)} %all-gather.2.cloned.1.call-done, f32[3072]{0:T(1024)} %param.17), kind=kOutput, calls=%fused_computation.25 | convolution fusion | flops 3626237952 | bytes 12988416 | tf_op jit(solution)/shard_map/dot_general | solution.py:89
  (92 shorter events, 68.6 us)
Async XLA Ops:
  6.5 375.4 %all-gather.2.cloned.1.call-start = ((), (), s32[]{:S(2)}) async-start(), calls=%async_computation | async-start | bytes 10027008 | tf_op jit(solution)/shard_map/all_gather | solution.py:91
  9.4 104.6 %collective-permute-start.3 = (bf16[384,3072]{1,0:T(8,128)(2,1)S(1)}, bf16[384,3072]{1,0:T(8,128)(2,1)S(1)}, u32[]{:S(2)}, u32[]{:S(2)}) collective-permute-start(bf16[384,3072]{1,0:T(8,128)(2,1)S(1)} %constant_dynamic-update-slice_fusion), channel_id=1, source_target_pairs={{0,8},{1,9},{2,10},{3,11},{4,12},{5,13},{6,14},{7,15},{8,0},{9,1},... | collective-permute-start | bytes 7077896 | tf_op jit(solution)/shard_map/ppermute | solution.py:50
  114.0 3.0 copy-start
  116.9 140.0 %collective-permute-start.4 = (bf16[2,384,3072]{2,1,0:T(8,128)(2,1)}, bf16[2,384,3072]{2,1,0:T(8,128)(2,1)}, u32[]{:S(2)}, u32[]{:S(2)}) collective-permute-start(bf16[2,384,3072]{2,1,0:T(8,128)(2,1)} %pad_maximum_fusion.1), channel_id=1, source_target_pairs={{0,1},{1,2},{2,3},{3,4},{4,5},{5,6},{6,7},{8,9},{9,10},{10,11},{11... | collective-permute-start | bytes 14155784 | tf_op jit(solution)/shard_map/ppermute | solution.py:59
  120.5 136.4 %collective-permute-start.5 = (bf16[2,384,3072]{2,1,0:T(8,128)(2,1)}, bf16[2,384,3072]{2,1,0:T(8,128)(2,1)}, u32[]{:S(2)}, u32[]{:S(2)}) collective-permute-start(bf16[2,384,3072]{2,1,0:T(8,128)(2,1)} %pad_maximum_fusion.1), channel_id=1, source_target_pairs={{1,0},{2,1},{3,2},{4,3},{5,4},{6,5},{7,6},{9,8},{10,9},{11,10},{12... | collective-permute-start | bytes 14155784 | tf_op jit(solution)/shard_map/ppermute | solution.py:60
  122.4 3.9 collective-permute-start
  127.1 96.1 %collective-permute-start.1 = (s32[2]{0:T(128)S(1)}, s32[2]{0:T(128)S(1)}, u32[]{:S(2)}, u32[]{:S(2)}) collective-permute-start(s32[2]{0:T(128)S(1)} %pad_add_fusion), channel_id=1, source_target_pairs={{0,1},{1,2},{2,3},{3,4},{4,5},{5,6},{6,7},{8,9},{9,10},{10,11},{11... | collective-permute-start | bytes 32 | tf_op jit(solution)/shard_map/ppermute | solution.py:59
  131.4 124.1 %collective-permute-start.2 = (s32[2]{0:T(128)S(1)}, s32[2]{0:T(128)S(1)}, u32[]{:S(2)}, u32[]{:S(2)}) collective-permute-start(s32[2]{0:T(128)S(1)} %pad_add_fusion), channel_id=1, source_target_pairs={{1,0},{2,1},{3,2},{4,3},{5,4},{6,5},{7,6},{9,8},{10,9},{11,10},{12... | collective-permute-start | bytes 32 | tf_op jit(solution)/shard_map/ppermute | solution.py:60
  256.9 13.1 %copy-start.1 = (s32[12,2]{0,1:T(2,128)S(1)}, s32[12,2]{0,1:T(2,128)}, u32[]{:S(2)}) copy-start(s32[12,2]{0,1:T(2,128)} %param.15) | copy-start | bytes 292
Sparse Core Ops, SparseCore 0:
  122.6 120.7 all-gather.1
